TPU v7x, 128 devices: a whole 4x4x4 slice. The times are simulated.
128 devices in a mesh: row: 64 (over y, z, x_lo, core), rep: 2 (over x_hi).
Axes of the slice: x: 4 (x_hi: 2, x_lo: 2; x = x_hi * 2 + x_lo), y: 4, z: 4, core: 2. Of those that a mesh axis runs over, the one named last changes fastest.
Arguments:
- out_grad: bfloat16 [65536, 256], P(('row', 'rep')), may hold values from -6 to 6
- relu_mask: int32 [65536, 256], P(('row', 'rep')), may hold values 0 or 1
- features: bfloat16 [65536, 256], P('row'), may hold values from -6 to 6
- weight: bfloat16 [256, 256], replicated, may hold values from -0.375 to 0.375
- tile_cols: int32 [512, 128], P('row', 'rep'), may hold values from 0 to 255, as said below
- tile_counts: int32 [512, 2], P('row', 'rep'), may hold values from 1 to 64
- tile_values: bfloat16 [512, 128, 128, 128], P('row', 'rep')
Outputs:
- grad_in: bfloat16 [65536, 256], P(('row', 'rep'))
- grad_weight: float32 [256, 256], replicated
Inputs may be any that keep to these rules, and one draw needn't show every extreme that they name: `tile_cols`: the 64 entries of one row tile and one index of rep are distinct column tiles.
All inputs are finite; a program needn't handle non-finite values. No bound on the sum of `relu_mask` on one device may be relied on, other than what follows from the above.
Results may differ from a plain program's by a relative error of at most 0.0049.
Values may be sent and summed in bfloat16 or wider, within the bound.
No kernel may reach another device: no remote copies, remote signals or barrier semaphores. Data moves between devices by JAX's collectives and lax.ppermute only.
A program may use at most 320 MiB of HBM per device.

v0:
```python
import math
import jax
import jax.numpy as jnp
from jax import lax
from jax.sharding import PartitionSpec as P

AXES = ("row", "rep")
CORE_BIT = 1
DOUBLING_STAGES = ((2, 0), (3, 4), (5, 6))


def xor_pairs(count, mask):
    return [(i, i ^ mask) for i in range(count)]


def group_mask(d, bits):
    return sum(((d >> i & 1) << b for i, b in enumerate(bits)))


def group_pos(idx, bits):
    return sum(((idx >> b & 1) << i for i, b in enumerate(bits)))


def butterfly_sum(x):
    count = lax.axis_size("row") * lax.axis_size("rep")
    idx = lax.axis_index(AXES)
    core = idx >> CORE_BIT & 1
    core_mask = 1 << CORE_BIT
    parts = x.reshape(2, x.shape[0] // 2, *x.shape[1:])
    mine = jnp.take(parts, core, axis=0)
    other = lax.ppermute(jnp.take(parts, 1 - core, axis=0), AXES, xor_pairs(count, core_mask))
    buf = jnp.where(core == 0, mine + other, other + mine)
    for bits in DOUBLING_STAGES:
        m = 1 << len(bits)
        pos = group_pos(idx, bits)
        got = [buf] + [
            lax.ppermute(buf, AXES, xor_pairs(count, group_mask(d, bits))) for d in range(1, m)
        ]
        ordered = jnp.take(jnp.stack(got), jnp.arange(m, dtype=jnp.int32) ^ pos, axis=0)
        buf = ordered[0]
        for j in range(1, m):
            buf = buf + ordered[j]
    got = lax.ppermute(buf, AXES, xor_pairs(count, core_mask))
    return jnp.where(core == 0, jnp.concatenate([buf, got]), jnp.concatenate([got, buf]))


def shards(out_grad, relu_mask, features, weight, tile_cols, tile_counts, tile_values):
    own_rows, feature_width = out_grad.shape
    row_tiles, most_slots = tile_cols.shape
    tile_size = tile_values.shape[-1]
    block_tiles = own_rows // tile_size
    column_tiles = block_tiles * lax.axis_size("row")
    gated = out_grad * relu_mask.astype(jnp.bfloat16)
    active = jnp.arange(most_slots, dtype=jnp.int32)[None, :] < tile_counts
    gathered = lax.all_gather(gated, "row", axis=0, tiled=True)
    grad_tiles = gathered.reshape(column_tiles, tile_size, feature_width)
    picked = jnp.take(grad_tiles, tile_cols, axis=0)
    picked = jnp.where(active[:, :, None, None], picked, jnp.zeros((), jnp.bfloat16))
    partial_sum = jnp.einsum(
        "tsab,tsbf->taf", tile_values, picked, preferred_element_type=jnp.float32
    )
    partial_sum = partial_sum.reshape(row_tiles * tile_size, feature_width)
    node_count = own_rows * lax.axis_size("row") * lax.axis_size("rep")
    normalizer = 1.0 / math.sqrt(node_count)
    weight_term = jnp.dot(
        features.astype(jnp.float32).T, partial_sum, precision=lax.Precision.HIGHEST
    )
    grad_weight = butterfly_sum(weight_term * normalizer)
    rep = lax.axis_index("rep")
    halves = partial_sum.reshape(2, own_rows, feature_width)
    other = lax.ppermute(jnp.take(halves, 1 - rep, axis=0), "rep", [(0, 1), (1, 0)])
    propagated = jnp.take(halves, rep, axis=0) + other
    grad_in = jnp.dot(
        propagated.astype(jnp.bfloat16), weight.T, preferred_element_type=jnp.float32
    ).astype(jnp.bfloat16)
    return (grad_in, grad_weight)


def solution(mesh):
    in_specs = (
        P(("row", "rep"), None),
        P(("row", "rep"), None),
        P("row", None),
        P(),
        P("row", "rep"),
        P("row", "rep"),
        P("row", "rep", None, None),
    )
    out_specs = (P(("row", "rep"), None), P())
    return jax.shard_map(shards, mesh=mesh, in_specs=in_specs, out_specs=out_specs, check_vma=False)
```

profile of v0, /device:TPU:1, one launch (start us, length us, event | category | flops | bytes accessed | tf_op | source)
XLA Modules:
  0.0 218.2 jit_solution(8378743402661240332)
XLA Ops:
  7.2 1.9 convert_multiply_fusion
  9.2 0.7 compare_select_fusion
  10.0 0.8 iota_compare_fusion
  10.8 125.0 %all-gather.2.cloned.1.call-done = bf16[32768,256]{1,0:T(8,128)(2,1)} async-done(((bf16[512,256]{1,0:T(8,128)(2,1)}), bf16[32768,256]{1,0:T(8,128)(2,1)}) %all-gather.2.cloned.1.call-update) | async-done | bytes 16777232 | tf_op jit(solution)/shard_map/all_gather | solution.py:55
  135.8 21.9 %gather_fusion = bf16[512,128,256]{2,1,0:T(8,128)(2,1)} fusion(bf16[256,128,256]{2,1,0:T(8,128)(2,1)} %bitcast.45, s32[1024]{0:T(1024)S(1)} %pad_clamp_fusion.3), kind=kCustom, calls=%fused_computation.3 | custom fusion | bytes 67110912 | tf_op jit(solution)/shard_map/jit(_take)/gather | solution.py:57
  157.7 17.5 %fusion = f32[8,256,128,1]{1,2,3,0:T(8,128)S(1)} fusion(bf16[8,64,128,128]{3,2,1,0:T(8,128)(2,1)} %param.19, bf16[8,64,128,256]{3,2,1,0:T(8,128)(2,1)} %bitcast.46, pred[8,64]{1,0:T(8,128)(4,1)S(1)} %get-tuple-element.28, pred[8,64]{1,0:T(8,128)(4,1)S(1)} %get-tuple-element.27), kind=kOutput, calls=%fused_computation.4 | convolution fusion | flops 4328521728 | bytes 51381248 | tf_op jit(solution)/shard_map/tsab,tsbf->taf/dot_general | solution.py:59
  175.2 0.8 convolution_multiply_fusion
  176.4 1.0 collective-permute-done.1
  177.5 1.9 collective-permute-start.4
  179.4 0.6 collective-permute-start.3
  180.0 0.8 collective-permute-start.2
  180.9 2.3 %collective-permute-start = (f32[512,256]{1,0:T(8,128)S(1)}, f32[512,256]{1,0:T(8,128)}, u32[]{:S(2)}, u32[]{:S(2)}) collective-permute-start(f32[512,256]{1,0:T(8,128)S(1)} %select_bitcast_fusion), channel_id=1, source_target_pairs={{0,1},{1,0},{2,3},{3,2},{4,5},{5,4},{6,7},{7,6},{8,9},{9,8},{10,11... | collective-permute-start | bytes 1572872 | tf_op jit(solution)/shard_map/ppermute | solution.py:71
  183.2 1.1 collective-permute-done.4
  184.2 1.3 collective-permute-done.3
  185.5 1.3 collective-permute-done.2
  186.8 0.6 gather_fusion.1
  187.6 1.3 collective-permute-start.7
  188.9 1.3 collective-permute-start.6
  190.2 0.8 collective-permute-start.5
  190.9 2.1 collective-permute-done.7
  193.1 1.5 collective-permute-done.6
  194.6 0.5 collective-permute-done.5
  195.1 0.6 gather_fusion.2
  195.8 1.4 collective-permute-start.10
  197.3 1.0 collective-permute-start.9
  198.3 0.9 collective-permute-start.8
  199.2 1.7 collective-permute-done.10
  201.0 1.6 collective-permute-done.9
  203.0 0.6 gather_fusion.3
  203.7 4.9 %collective-permute-start.11 = (f32[128,256]{1,0:T(8,128)S(1)}, f32[128,256]{1,0:T(8,128)S(1)}, u32[]{:S(2)}, u32[]{:S(2)}) collective-permute-start(f32[128,256]{1,0:T(8,128)S(1)} %fusion.11), channel_id=1, source_target_pairs={{0,2},{1,3},{2,0},{3,1},{4,6},{5,7},{6,4},{7,5},{8,10},{9,11},{10,... | collective-permute-start | bytes 393224 | tf_op jit(solution)/shard_map/ppermute | solution.py:43
  208.6 2.0 convolution_convert_fusion
  210.6 0.7 maximum_select_fusion
  (34 shorter events, 1.6 us)
Async XLA Ops:
  7.2 168.1 %copy-start = (bf16[1024,256]{1,0:T(8,128)(2,1)S(1)}, bf16[1024,256]{1,0:T(8,128)(2,1)}, u32[]{:S(2)}) copy-start(bf16[1024,256]{1,0:T(8,128)(2,1)} %param.15) | copy-start | bytes 1572868
  7.2 128.6 %all-gather.2.cloned.1.call-start = ((), (), s32[]{:S(2)}) async-start(), calls=%async_computation | async-start | bytes 17039360 | tf_op jit(solution)/shard_map/all_gather | solution.py:55
  157.7 50.9 %copy-start.1 = (bf16[256,256]{1,0:T(8,128)(2,1)S(1)}, bf16[256,256]{1,0:T(8,128)(2,1)}, u32[]{:S(2)}) copy-start(bf16[256,256]{1,0:T(8,128)(2,1)} %param.16) | copy-start | bytes 393220
  176.1 1.4 collective-permute-start.1
  177.5 6.7 %collective-permute-start.4 = (f32[128,256]{1,0:T(8,128)S(1)}, f32[128,256]{1,0:T(8,128)S(1)}, u32[]{:S(2)}, u32[]{:S(2)}) collective-permute-start(f32[128,256]{1,0:T(8,128)S(1)} %bitcast_add_fusion.1), channel_id=1, source_target_pairs={{0,5},{1,4},{2,7},{3,6},{4,1},{5,0},{6,3},{7,2},{8,13},{9,12},{10,... | collective-permute-start | bytes 393224 | tf_op jit(solution)/shard_map/ppermute | solution.py:37
  179.4 6.1 %collective-permute-start.3 = (f32[128,256]{1,0:T(8,128)S(1)}, f32[128,256]{1,0:T(8,128)S(1)}, u32[]{:S(2)}, u32[]{:S(2)}) collective-permute-start(f32[128,256]{1,0:T(8,128)S(1)} %bitcast_add_fusion.1), channel_id=1, source_target_pairs={{0,1},{1,0},{2,3},{3,2},{4,5},{5,4},{6,7},{7,6},{8,9},{9,8},{10,11... | collective-permute-start | bytes 393224 | tf_op jit(solution)/shard_map/ppermute | solution.py:37
  180.0 6.8 %collective-permute-start.2 = (f32[128,256]{1,0:T(8,128)S(1)}, f32[128,256]{1,0:T(8,128)S(1)}, u32[]{:S(2)}, u32[]{:S(2)}) collective-permute-start(f32[128,256]{1,0:T(8,128)S(1)} %bitcast_add_fusion.1), channel_id=1, source_target_pairs={{0,4},{1,5},{2,6},{3,7},{4,0},{5,1},{6,2},{7,3},{8,12},{9,13},{10,... | collective-permute-start | bytes 393224 | tf_op jit(solution)/shard_map/ppermute | solution.py:37
  180.9 27.7 %collective-permute-start = (f32[512,256]{1,0:T(8,128)S(1)}, f32[512,256]{1,0:T(8,128)}, u32[]{:S(2)}, u32[]{:S(2)}) collective-permute-start(f32[512,256]{1,0:T(8,128)S(1)} %select_bitcast_fusion), channel_id=1, source_target_pairs={{0,1},{1,0},{2,3},{3,2},{4,5},{5,4},{6,7},{7,6},{8,9},{9,8},{10,11... | collective-permute-start | bytes 1572872 | tf_op jit(solution)/shard_map/ppermute | solution.py:71
  187.6 5.5 %collective-permute-start.7 = (f32[128,256]{1,0:T(8,128)S(1)}, f32[128,256]{1,0:T(8,128)S(1)}, u32[]{:S(2)}, u32[]{:S(2)}) collective-permute-start(f32[128,256]{1,0:T(8,128)S(1)} %fusion.21), channel_id=1, source_target_pairs={{0,24},{1,25},{2,26},{3,27},{4,28},{5,29},{6,30},{7,31},{8,16},{9,... | collective-permute-start | bytes 393224 | tf_op jit(solution)/shard_map/ppermute | solution.py:37
  188.9 5.7 %collective-permute-start.6 = (f32[128,256]{1,0:T(8,128)S(1)}, f32[128,256]{1,0:T(8,128)S(1)}, u32[]{:S(2)}, u32[]{:S(2)}) collective-permute-start(f32[128,256]{1,0:T(8,128)S(1)} %fusion.21), channel_id=1, source_target_pairs={{0,16},{1,17},{2,18},{3,19},{4,20},{5,21},{6,22},{7,23},{8,24},{9,... | collective-permute-start | bytes 393224 | tf_op jit(solution)/shard_map/ppermute | solution.py:37
  190.2 4.9 %collective-permute-start.5 = (f32[128,256]{1,0:T(8,128)S(1)}, f32[128,256]{1,0:T(8,128)S(1)}, u32[]{:S(2)}, u32[]{:S(2)}) collective-permute-start(f32[128,256]{1,0:T(8,128)S(1)} %fusion.21), channel_id=1, source_target_pairs={{0,8},{1,9},{2,10},{3,11},{4,12},{5,13},{6,14},{7,15},{8,0},{9,1},... | collective-permute-start | bytes 393224 | tf_op jit(solution)/shard_map/ppermute | solution.py:37
  195.8 5.1 %collective-permute-start.10 = (f32[128,256]{1,0:T(8,128)S(1)}, f32[128,256]{1,0:T(8,128)S(1)}, u32[]{:S(2)}, u32[]{:S(2)}) collective-permute-start(f32[128,256]{1,0:T(8,128)S(1)} %fusion.20), channel_id=1, source_target_pairs={{0,96},{1,97},{2,98},{3,99},{4,100},{5,101},{6,102},{7,103},{8,104... | collective-permute-start | bytes 393224 | tf_op jit(solution)/shard_map/ppermute | solution.py:37
  197.3 5.3 %collective-permute-start.9 = (f32[128,256]{1,0:T(8,128)S(1)}, f32[128,256]{1,0:T(8,128)S(1)}, u32[]{:S(2)}, u32[]{:S(2)}) collective-permute-start(f32[128,256]{1,0:T(8,128)S(1)} %fusion.20), channel_id=1, source_target_pairs={{0,64},{1,65},{2,66},{3,67},{4,68},{5,69},{6,70},{7,71},{8,72},{9,... | collective-permute-start | bytes 393224 | tf_op jit(solution)/shard_map/ppermute | solution.py:37
  198.3 4.6 %collective-permute-start.8 = (f32[128,256]{1,0:T(8,128)S(1)}, f32[128,256]{1,0:T(8,128)S(1)}, u32[]{:S(2)}, u32[]{:S(2)}) collective-permute-start(f32[128,256]{1,0:T(8,128)S(1)} %fusion.20), channel_id=1, source_target_pairs={{0,32},{1,33},{2,34},{3,35},{4,36},{5,37},{6,38},{7,39},{8,40},{9,... | collective-permute-start | bytes 393224 | tf_op jit(solution)/shard_map/ppermute | solution.py:37
  203.7 6.9 %collective-permute-start.11 = (f32[128,256]{1,0:T(8,128)S(1)}, f32[128,256]{1,0:T(8,128)S(1)}, u32[]{:S(2)}, u32[]{:S(2)}) collective-permute-start(f32[128,256]{1,0:T(8,128)S(1)} %fusion.11), channel_id=1, source_target_pairs={{0,2},{1,3},{2,0},{3,1},{4,6},{5,7},{6,4},{7,5},{8,10},{9,11},{10,... | collective-permute-start | bytes 393224 | tf_op jit(solution)/shard_map/ppermute | solution.py:43
Sparse Core Ops, SparseCore 0:
  10.3 125.4 all-gather.1
where the time goes:
time: 218 us
  waiting for transfers between devices  138 us (63%)
  local copies, waits for them, and re-layouts  23.8 us (11%)
  matrix products  20.3 us (9%)
  starting transfers between devices  17.6 us (8%)
  between operations  14.2 us (7%)
  other arithmetic  4.84 us (2%)
    all_gather x1, waiting for transfers between devices, shards(): gathered = lax.all_gather(gated, 'row', axis=0, tiled=True)  125 us
    gather x1, local copies, waits for them, and re-layouts, shards(): picked = jnp.take(grad_tiles, tile_cols, axis=0)  21.9 us
    dot_general x1, matrix products, shards(): jnp.einsum('tsab,tsbf->taf', tile_values, picked, preferred_element_type=...  17.5 us
    ppermute x9, waiting for transfers between devices, butterfly_sum(): lax.ppermute(buf, AXES, xor_pairs(count, group_mask(d, bits)))  11.4 us
    ppermute x9, starting transfers between devices, butterfly_sum(): lax.ppermute(buf, AXES, xor_pairs(count, group_mask(d, bits)))  10 us
    ppermute x1, starting transfers between devices, butterfly_sum(): got = lax.ppermute(buf, AXES, xor_pairs(count, core_mask))  4.89 us
  transfers between devices with their start and end apart: 13, of which 11 were waited for; matrix products, arithmetic and copies ran while one was open for 3% of the time, Pallas kernels for 0%

commit v1 on v0

--- a/solution.py
+++ b/solution.py
@@ -52,7 +52,9 @@
     column_tiles = block_tiles * lax.axis_size("row")
     gated = out_grad * relu_mask.astype(jnp.bfloat16)
     active = jnp.arange(most_slots, dtype=jnp.int32)[None, :] < tile_counts
-    gathered = lax.all_gather(gated, "row", axis=0, tiled=True)
+    gathered = jnp.concatenate(
+        lax.all_to_all(jnp.stack([gated] * lax.axis_size("row")), "row", 0, 0), axis=0
+    )
     grad_tiles = gathered.reshape(column_tiles, tile_size, feature_width)
     picked = jnp.take(grad_tiles, tile_cols, axis=0)
     picked = jnp.where(active[:, :, None, None], picked, jnp.zeros((), jnp.bfloat16))

time: 218 us -> 352 us (1.61)
  waiting for transfers between devices: 138 us -> 221 us
  starting transfers between devices: 17.6 us -> 76.8 us
  between operations: 14.2 us -> 0.9 us
  local copies, waits for them, and re-layouts: 23.8 us -> 29.7 us
    all_to_all x0 -> x1, waiting for transfers between devices: none -> 207 us  [shards(): lax.all_to_all(jnp.stack([gated] * lax.axis_size('row')), 'row', 0, 0)]
    all_gather x1 -> x0, waiting for transfers between devices: 125 us -> none  [shards(): gathered = lax.all_gather(gated, 'row', axis=0, tiled=True)]
    ppermute x9, starting transfers between devices: 10 us -> 58.7 us  [butterfly_sum(): lax.ppermute(buf, AXES, xor_pairs(count, group_mask(d, bits)))]
    all_to_all x0 -> x1, starting transfers between devices: none -> 11.1 us  [shards(): lax.all_to_all(jnp.stack([gated] * lax.axis_size('row')), 'row', 0, 0)]
    another operation x0 -> x1, local copies, waits for them, and re-layouts: none -> 5.95 us  [shards(): jnp.stack([gated] * lax.axis_size('row'))]
  transfers between devices with their start and end apart: 13 -> 13, of which waited for: 11 -> 9; matrix products, arithmetic and copies ran while one was open for 3% -> 1% of each run, Pallas kernels for 0% -> 0%
where the time goes in v1:
time: 352 us; the launch traced here: 351 us
  waiting for transfers between devices  221 us (63%)
  starting transfers between devices  76.8 us (22%)
  local copies, waits for them, and re-layouts  29.7 us (8%)
  matrix products  20.3 us (6%)
    all_to_all x1, waiting for transfers between devices, shards(): lax.all_to_all(jnp.stack([gated] * lax.axis_size('row')), 'row', 0, 0)  207 us
    ppermute x9, starting transfers between devices, butterfly_sum(): lax.ppermute(buf, AXES, xor_pairs(count, group_mask(d, bits)))  58.7 us
    gather x1, local copies, waits for them, and re-layouts, shards(): picked = jnp.take(grad_tiles, tile_cols, axis=0)  21.9 us
    dot_general x1, matrix products, shards(): jnp.einsum('tsab,tsbf->taf', tile_values, picked, preferred_element_type=...  17.5 us
    ppermute x9, waiting for transfers between devices, butterfly_sum(): lax.ppermute(buf, AXES, xor_pairs(count, group_mask(d, bits)))  12.8 us
    all_to_all x1, starting transfers between devices, shards(): lax.all_to_all(jnp.stack([gated] * lax.axis_size('row')), 'row', 0, 0)  11.1 us
  transfers between devices with their start and end apart: 13, of which 9 were waited for; matrix products, arithmetic and copies ran while one was open for 1% of the time, Pallas kernels for 0%

profile of v1, /device:TPU:1, one launch (start us, length us, event | category | flops | bytes accessed | tf_op | source)
XLA Modules:
  0.0 351.3 jit_solution(10029444392687819280)
XLA Ops:
  0.7 1.2 convert_multiply_fusion
  1.9 6.0 %stack.28 = bf16[64,512,256]{2,1,0:T(8,128)(2,1)} broadcast(bf16[512,256]{1,0:T(8,128)(2,1)S(1)} %convert_multiply_fusion), dimensions={1,2} | broadcast | bytes 17039360 | tf_op jit(solution)/shard_map/stack | solution.py:56
  7.8 11.1 %all-to-all-start = ((bf16[64,512,256]{2,1,0:T(8,128)(2,1)}), bf16[64,512,256]{2,1,0:T(8,128)(2,1)}, u32[]{:S(2)}, u32[]{:S(2)}) async-start(bf16[64,512,256]{2,1,0:T(8,128)(2,1)} %stack.28), calls=%async_computation | async-start | bytes 33554432 | tf_op jit(solution)/shard_map/all_to_all | solution.py:56
  19.2 207.0 %all-to-all-done = bf16[64,512,256]{2,1,0:T(8,128)(2,1)} async-done(((bf16[64,512,256]{2,1,0:T(8,128)(2,1)}), bf16[64,512,256]{2,1,0:T(8,128)(2,1)}, u32[]{:S(2)}, u32[]{:S(2)}) %all-to-all-start) | async-done | bytes 16777248 | tf_op jit(solution)/shard_map/all_to_all | solution.py:56
  226.2 21.9 %gather_fusion = bf16[512,128,256]{2,1,0:T(8,128)(2,1)} fusion(bf16[256,128,256]{2,1,0:T(8,128)(2,1)} %bitcast.1, s32[1024]{0:T(1024)S(1)} %pad_clamp_fusion.3), kind=kCustom, calls=%fused_computation.3 | custom fusion | bytes 67110912 | tf_op jit(solution)/shard_map/jit(_take)/gather | solution.py:59
  248.2 17.5 %fusion = f32[8,256,128,1]{1,2,3,0:T(8,128)S(1)} fusion(bf16[8,64,128,128]{3,2,1,0:T(8,128)(2,1)} %param.19, bf16[8,64,128,256]{3,2,1,0:T(8,128)(2,1)} %bitcast.45, pred[8,64]{1,0:T(8,128)(4,1)S(1)} %get-tuple-element.28, pred[8,64]{1,0:T(8,128)(4,1)S(1)} %get-tuple-element.27), kind=kOutput, calls=%fused_computation.4 | convolution fusion | flops 4328521728 | bytes 51381248 | tf_op jit(solution)/shard_map/tsab,tsbf->taf/dot_general | solution.py:61
  265.7 0.8 convolution_multiply_fusion
  266.5 1.2 collective-permute-start.1
  267.7 1.0 collective-permute-done.1
  268.7 38.8 %collective-permute-start.4 = (f32[128,256]{1,0:T(8,128)S(1)}, f32[128,256]{1,0:T(8,128)S(1)}, u32[]{:S(2)}, u32[]{:S(2)}) collective-permute-start(f32[128,256]{1,0:T(8,128)S(1)} %bitcast_add_fusion.1), channel_id=1, source_target_pairs={{0,5},{1,4},{2,7},{3,6},{4,1},{5,0},{6,3},{7,2},{8,13},{9,12},{10,... | collective-permute-start | bytes 393224 | tf_op jit(solution)/shard_map/ppermute | solution.py:37
  307.6 0.5 collective-permute-start.3
  308.1 0.1 collective-permute-start.2
  308.3 2.4 collective-permute-start
  310.7 2.4 collective-permute-done.4
  313.1 0.4 collective-permute-done.3
  313.5 0.8 collective-permute-done.2
  314.3 0.6 gather_fusion.1
  314.9 0.1 broadcast_select_fusion.2
  315.1 0.1 collective-permute-start.7
  315.2 15.3 %collective-permute-start.6 = (f32[128,256]{1,0:T(8,128)S(1)}, f32[128,256]{1,0:T(8,128)S(1)}, u32[]{:S(2)}, u32[]{:S(2)}) collective-permute-start(f32[128,256]{1,0:T(8,128)S(1)} %fusion.21), channel_id=1, source_target_pairs={{0,16},{1,17},{2,18},{3,19},{4,20},{5,21},{6,22},{7,23},{8,24},{9,... | collective-permute-start | bytes 393224 | tf_op jit(solution)/shard_map/ppermute | solution.py:37
  330.5 2.3 collective-permute-done.6
  332.8 2.5 collective-permute-done.5
  335.4 0.6 gather_fusion.2
  336.0 0.1 broadcast_select_fusion.1
  336.2 3.8 %collective-permute-start.9 = (f32[128,256]{1,0:T(8,128)S(1)}, f32[128,256]{1,0:T(8,128)S(1)}, u32[]{:S(2)}, u32[]{:S(2)}) collective-permute-start(f32[128,256]{1,0:T(8,128)S(1)} %fusion.20), channel_id=1, source_target_pairs={{0,64},{1,65},{2,66},{3,67},{4,68},{5,69},{6,70},{7,71},{8,72},{9,... | collective-permute-start | bytes 393224 | tf_op jit(solution)/shard_map/ppermute | solution.py:37
  340.1 2.6 collective-permute-done.10
  342.7 1.7 collective-permute-done.8
  344.4 0.6 gather_fusion.3
  345.0 0.1 broadcast_select_fusion
  345.2 3.4 collective-permute-start.11
  348.6 2.0 convolution_convert_fusion
  350.6 0.7 maximum_select_fusion
  (38 shorter events, 0.7 us)
Async XLA Ops:
  0.6 265.1 %copy-start = (bf16[1024,256]{1,0:T(8,128)(2,1)S(1)}, bf16[1024,256]{1,0:T(8,128)(2,1)}, u32[]{:S(2)}) copy-start(bf16[1024,256]{1,0:T(8,128)(2,1)} %param.15) | copy-start | bytes 1572868
  0.6 18.3 %copy-start.2 = (s32[8,64]{1,0:T(8,128)S(1)}, s32[8,64]{1,0:T(8,128)}, u32[]{:S(2)}) copy-start(s32[8,64]{1,0:T(8,128)} %param.17) | copy-start | bytes 6148
  0.7 18.5 %copy-start.3 = (s32[8,1]{0,1:T(1,128)S(1)}, s32[8,1]{0,1:T(1,128)}, u32[]{:S(2)}) copy-start(s32[8,1]{0,1:T(1,128)} %param.18) | copy-start | bytes 100
  7.8 218.4 %all-to-all-start = ((bf16[64,512,256]{2,1,0:T(8,128)(2,1)}), bf16[64,512,256]{2,1,0:T(8,128)(2,1)}, u32[]{:S(2)}, u32[]{:S(2)}) async-start(bf16[64,512,256]{2,1,0:T(8,128)(2,1)} %stack.28), calls=%async_computation | async-start | bytes 33554432 | tf_op jit(solution)/shard_map/all_to_all | solution.py:56
  248.2 100.4 %copy-start.1 = (bf16[256,256]{1,0:T(8,128)(2,1)S(1)}, bf16[256,256]{1,0:T(8,128)(2,1)}, u32[]{:S(2)}) copy-start(bf16[256,256]{1,0:T(8,128)(2,1)} %param.16) | copy-start | bytes 393220
  266.5 2.2 collective-permute-start.1
  268.7 44.3 %collective-permute-start.4 = (f32[128,256]{1,0:T(8,128)S(1)}, f32[128,256]{1,0:T(8,128)S(1)}, u32[]{:S(2)}, u32[]{:S(2)}) collective-permute-start(f32[128,256]{1,0:T(8,128)S(1)} %bitcast_add_fusion.1), channel_id=1, source_target_pairs={{0,5},{1,4},{2,7},{3,6},{4,1},{5,0},{6,3},{7,2},{8,13},{9,12},{10,... | collective-permute-start | bytes 393224 | tf_op jit(solution)/shard_map/ppermute | solution.py:37
  307.6 5.9 %collective-permute-start.3 = (f32[128,256]{1,0:T(8,128)S(1)}, f32[128,256]{1,0:T(8,128)S(1)}, u32[]{:S(2)}, u32[]{:S(2)}) collective-permute-start(f32[128,256]{1,0:T(8,128)S(1)} %bitcast_add_fusion.1), channel_id=1, source_target_pairs={{0,1},{1,0},{2,3},{3,2},{4,5},{5,4},{6,7},{7,6},{8,9},{9,8},{10,11... | collective-permute-start | bytes 393224 | tf_op jit(solution)/shard_map/ppermute | solution.py:37
  308.1 6.2 %collective-permute-start.2 = (f32[128,256]{1,0:T(8,128)S(1)}, f32[128,256]{1,0:T(8,128)S(1)}, u32[]{:S(2)}, u32[]{:S(2)}) collective-permute-start(f32[128,256]{1,0:T(8,128)S(1)} %bitcast_add_fusion.1), channel_id=1, source_target_pairs={{0,4},{1,5},{2,6},{3,7},{4,0},{5,1},{6,2},{7,3},{8,12},{9,13},{10,... | collective-permute-start | bytes 393224 | tf_op jit(solution)/shard_map/ppermute | solution.py:37
  308.3 40.3 %collective-permute-start = (f32[512,256]{1,0:T(8,128)S(1)}, f32[512,256]{1,0:T(8,128)}, u32[]{:S(2)}, u32[]{:S(2)}) collective-permute-start(f32[512,256]{1,0:T(8,128)S(1)} %select_bitcast_fusion), channel_id=1, source_target_pairs={{0,1},{1,0},{2,3},{3,2},{4,5},{5,4},{6,7},{7,6},{8,9},{9,8},{10,11... | collective-permute-start | bytes 1572872 | tf_op jit(solution)/shard_map/ppermute | solution.py:73
  315.1 15.4 %collective-permute-start.7 = (f32[128,256]{1,0:T(8,128)S(1)}, f32[128,256]{1,0:T(8,128)S(1)}, u32[]{:S(2)}, u32[]{:S(2)}) collective-permute-start(f32[128,256]{1,0:T(8,128)S(1)} %fusion.21), channel_id=1, source_target_pairs={{0,24},{1,25},{2,26},{3,27},{4,28},{5,29},{6,30},{7,31},{8,16},{9,... | collective-permute-start | bytes 393224 | tf_op jit(solution)/shard_map/ppermute | solution.py:37
  315.2 17.6 %collective-permute-start.6 = (f32[128,256]{1,0:T(8,128)S(1)}, f32[128,256]{1,0:T(8,128)S(1)}, u32[]{:S(2)}, u32[]{:S(2)}) collective-permute-start(f32[128,256]{1,0:T(8,128)S(1)} %fusion.21), channel_id=1, source_target_pairs={{0,16},{1,17},{2,18},{3,19},{4,20},{5,21},{6,22},{7,23},{8,24},{9,... | collective-permute-start | bytes 393224 | tf_op jit(solution)/shard_map/ppermute | solution.py:37
  330.5 4.9 %collective-permute-start.5 = (f32[128,256]{1,0:T(8,128)S(1)}, f32[128,256]{1,0:T(8,128)S(1)}, u32[]{:S(2)}, u32[]{:S(2)}) collective-permute-start(f32[128,256]{1,0:T(8,128)S(1)} %fusion.21), channel_id=1, source_target_pairs={{0,8},{1,9},{2,10},{3,11},{4,12},{5,13},{6,14},{7,15},{8,0},{9,1},... | collective-permute-start | bytes 393224 | tf_op jit(solution)/shard_map/ppermute | solution.py:37
  336.1 6.5 %collective-permute-start.10 = (f32[128,256]{1,0:T(8,128)S(1)}, f32[128,256]{1,0:T(8,128)S(1)}, u32[]{:S(2)}, u32[]{:S(2)}) collective-permute-start(f32[128,256]{1,0:T(8,128)S(1)} %fusion.20), channel_id=1, source_target_pairs={{0,96},{1,97},{2,98},{3,99},{4,100},{5,101},{6,102},{7,103},{8,104... | collective-permute-start | bytes 393224 | tf_op jit(solution)/shard_map/ppermute | solution.py:37
  336.2 6.4 %collective-permute-start.9 = (f32[128,256]{1,0:T(8,128)S(1)}, f32[128,256]{1,0:T(8,128)S(1)}, u32[]{:S(2)}, u32[]{:S(2)}) collective-permute-start(f32[128,256]{1,0:T(8,128)S(1)} %fusion.20), channel_id=1, source_target_pairs={{0,64},{1,65},{2,66},{3,67},{4,68},{5,69},{6,70},{7,71},{8,72},{9,... | collective-permute-start | bytes 393224 | tf_op jit(solution)/shard_map/ppermute | solution.py:37
  340.0 4.4 %collective-permute-start.8 = (f32[128,256]{1,0:T(8,128)S(1)}, f32[128,256]{1,0:T(8,128)S(1)}, u32[]{:S(2)}, u32[]{:S(2)}) collective-permute-start(f32[128,256]{1,0:T(8,128)S(1)} %fusion.20), channel_id=1, source_target_pairs={{0,32},{1,33},{2,34},{3,35},{4,36},{5,37},{6,38},{7,39},{8,40},{9,... | collective-permute-start | bytes 393224 | tf_op jit(solution)/shard_map/ppermute | solution.py:37
  345.2 5.4 %collective-permute-start.11 = (f32[128,256]{1,0:T(8,128)S(1)}, f32[128,256]{1,0:T(8,128)S(1)}, u32[]{:S(2)}, u32[]{:S(2)}) collective-permute-start(f32[128,256]{1,0:T(8,128)S(1)} %fusion.11), channel_id=1, source_target_pairs={{0,2},{1,3},{2,0},{3,1},{4,6},{5,7},{6,4},{7,5},{8,10},{9,11},{10,... | collective-permute-start | bytes 393224 | tf_op jit(solution)/shard_map/ppermute | solution.py:43
